TPU v7x, 256 devices: a whole 4x4x8 slice. The times are simulated.
256 devices in a mesh: dp: 4 (over y), section: 16 (over z, x_lo), tensor: 4 (over x_hi, core).
Axes of the slice: x: 4 (x_hi: 2, x_lo: 2; x = x_hi * 2 + x_lo), y: 4, z: 8, core: 2. Of those that a mesh axis runs over, the one named last changes fastest.
Arguments:
- saved_input: bfloat16 [16, 2, 512, 8192], P('section', None, ('dp', 'tensor')), may hold values from -6 to 6
- kv_grad: bfloat16 [16, 2, 512, 2048], P('section', None, 'dp', 'tensor'), may hold values from -1.5 to 1.5
- kv_weight: bfloat16 [16, 8192, 2048], P('section', 'dp', 'tensor'), may hold values from -0.0625 to 0.0625
- norm_gain: bfloat16 [16, 8192], P('section'), may hold values from 0.5 to 1.5
- top_grad: bfloat16 [2, 512, 8192], P(None, ('dp', 'tensor')), may hold values from -1.5 to 1.5
- noise_salt: int32 [1], replicated, may hold values from 0 to 1073741823
- step_counter: int32 [1], replicated, may hold values from 0 to 999999
Outputs:
- input_grads: bfloat16 [16, 2, 512, 8192], P('section', None, ('dp', 'tensor'))
- weight_grads: float32 [16, 8192, 2048], P('section', 'dp', 'tensor')
All inputs are finite; a program needn't handle non-finite values.
Results may differ from a plain program's by a relative error of at most 0.012.
Values may be sent and summed in bfloat16 or wider, within the bound.
No kernel may reach another device: no remote copies, remote signals or barrier semaphores. Data moves between devices by JAX's collectives and lax.ppermute only.
A program may use at most 128 MiB of HBM per device.

v0:
```python
import jax
import jax.numpy as jnp
from jax import lax
from jax.sharding import PartitionSpec as P


def mix_bits(salt, counter, layer, group, index):
    h = (
        index * jnp.int32(-1640531535)
        + salt * jnp.int32(374761393)
        + counter * jnp.int32(668265263)
    )
    h = h + layer * jnp.int32(-1028477379) + group * jnp.int32(1274126177)
    h = h ^ lax.shift_right_logical(h, jnp.int32(16))
    h = h * jnp.int32(2146121005)
    h = h ^ lax.shift_right_logical(h, jnp.int32(15))
    h = h * jnp.int32(-2073254261)
    h = h ^ lax.shift_right_logical(h, jnp.int32(16))
    return lax.shift_right_logical(h, jnp.int32(8)).astype(jnp.float32) * (1.0 / 16777216.0)


def dither(term, salt, counter, layer, group, index):
    noise = mix_bits(salt, counter, layer, group, index)
    moved = term * (1.0 + (noise - 0.5) * 0.5)
    return lax.optimization_barrier(moved.astype(jnp.bfloat16)).astype(jnp.float32)


def later_sum(branch_path):
    n_sec = lax.axis_size("section")
    m, t, d = branch_path.shape
    chunks = lax.all_to_all(
        branch_path.astype(jnp.bfloat16)[None], "section", 3, 0, tiled=True
    ).astype(jnp.float32)
    acc = jnp.zeros(chunks.shape[1:], jnp.float32)
    outs = [None] * n_sec
    for s in range(n_sec - 1, -1, -1):
        outs[s] = acc
        acc = acc + chunks[s]
    stacked = jnp.stack(outs).astype(jnp.bfloat16)
    back = lax.all_to_all(stacked, "section", 0, 3, tiled=True)
    return back[0].astype(jnp.float32)


def shards(saved_input, kv_grad, kv_weight, norm_gain, top_grad, noise_salt, step_counter):
    salt = noise_salt[0]
    counter = step_counter[0]
    layer = lax.axis_index("section")
    n_dp = lax.axis_size("dp")
    n_t = lax.axis_size("tensor")
    my_p = lax.axis_index("dp")
    my_t = lax.axis_index("tensor")
    cotan = kv_grad[0]
    weight = kv_weight[0]
    rows_p, width_t = weight.shape
    total_cols = width_t * n_t
    mb, tok_dev, d_model = saved_input.shape[1:]
    input_float = saved_input[0].astype(jnp.float32)
    inverse_scale = lax.rsqrt(jnp.mean(input_float * input_float, axis=-1, keepdims=True) + 1e-05)
    centered_input = input_float * inverse_scale
    gain_float = norm_gain[0].astype(jnp.float32)
    normed_values = (centered_input * gain_float).astype(jnp.bfloat16)
    cotan_all = lax.all_gather(cotan, "dp", axis=1, tiled=True)
    part = jnp.einsum("mtk,dk->mtd", cotan_all, weight, preferred_element_type=jnp.float32).astype(
        jnp.bfloat16
    )
    part = part.reshape(mb, n_dp * n_t, tok_dev, rows_p).transpose(1, 0, 2, 3)
    got = lax.all_to_all(part, ("dp", "tensor"), 0, 0, tiled=True)
    got = got.reshape(n_dp, n_t, mb, tok_dev, rows_p).astype(jnp.float32)
    normed_grad = got[:, 0]
    for t in range(1, n_t):
        normed_grad = normed_grad + got[:, t]
    normed_grad = normed_grad.transpose(1, 2, 0, 3).reshape(mb, tok_dev, d_model)
    hidden_gradient = normed_grad * gain_float
    branch_path = inverse_scale * (
        hidden_gradient
        - centered_input * jnp.mean(hidden_gradient * centered_input, axis=-1, keepdims=True)
    )
    later = later_sum(branch_path)
    grad_in = (top_grad.astype(jnp.float32) + branch_path + later).astype(jnp.bfloat16)
    nrm = normed_values.reshape(mb, tok_dev, n_dp, rows_p).transpose(2, 0, 1, 3)
    nrm = lax.all_to_all(nrm, "dp", 0, 0, tiled=True)
    nrm = lax.all_gather(nrm, "tensor", axis=0, tiled=False)
    cot = cotan_all.reshape(mb, n_dp, n_t, tok_dev, width_t)
    terms = jnp.einsum("tpmid,mptik->pdk", nrm, cot, preferred_element_type=jnp.float32)
    row_ids = my_p * jnp.int32(rows_p) + jnp.arange(rows_p, dtype=jnp.int32)
    index = (
        row_ids[:, None] * jnp.int32(total_cols)
        + my_t * jnp.int32(width_t)
        + jnp.arange(width_t, dtype=jnp.int32)[None, :]
    )
    wsum = jnp.zeros((rows_p, width_t), jnp.float32)
    for g in range(n_dp):
        wsum = wsum + dither(terms[g], salt, counter, layer, jnp.int32(g), index)
    return (grad_in[None], wsum[None])


def solution(mesh):
    placed = (
        P("section", None, ("dp", "tensor"), None),
        P("section", None, "dp", "tensor"),
        P("section", "dp", "tensor"),
        P("section", None),
        P(None, ("dp", "tensor"), None),
        P(),
        P(),
    )
    return jax.shard_map(
        shards,
        mesh=mesh,
        in_specs=placed,
        out_specs=(P("section", None, ("dp", "tensor"), None), P("section", "dp", "tensor")),
        check_vma=False,
    )
```

profile of v0, /device:TPU:8, one launch (start us, length us, event | category | flops | bytes accessed | tf_op | source)
XLA Modules:
  0.0 288.4 jit_solution(17948738188843804011)
XLA Ops:
  7.2 0.0 copy-start
  7.2 0.0 all-gather.5.cloned.1.call-start
  7.2 0.7 all-gather.5.cloned.1.call-update
  7.9 30.3 %all-gather.5.cloned.1.call-done = bf16[1,2,512,512]{3,2,1,0:T(8,128)(2,1)} async-done(((bf16[1,2,128,512]{3,2,1,0:T(8,128)(2,1)}), bf16[1,2,512,512]{3,2,1,0:T(8,128)(2,1)}) %all-gather.5.cloned.1.call-update) | async-done | bytes 1048592 | tf_op jit(solution)/shard_map/all_gather | solution.py:62
  38.2 0.0 copy-done
  38.2 3.6 %convolution_convert_fusion = bf16[2,512,2048]{2,1,0:T(8,128)(2,1)S(1)} fusion(bf16[1,2048,512]{2,1,0:T(8,128)(2,1)S(1)} %copy-done, bf16[1,2,512,512]{3,2,1,0:T(8,128)(2,1)} %all-gather.5.cloned.1.call-done), kind=kOutput, calls=%fused_computation.60 | convolution fusion | flops 2149580800 | bytes 7340032 | tf_op jit(solution)/shard_map/mtk,dk->mtd/dot_general | solution.py:63
  41.8 2.3 copy.237
  44.1 7.6 %all-to-all-start = ((bf16[16,2,32,2048]{3,2,1,0:T(8,128)(2,1)}), bf16[16,2,32,2048]{3,2,1,0:T(8,128)(2,1)}, u32[]{:S(2)}, u32[]{:S(2)}) async-start(bf16[16,2,32,2048]{3,2,1,0:T(8,128)(2,1)} %bitcast.145), calls=%async_computation | async-start | bytes 8388608 | tf_op jit(solution)/shard_map/all_to_all | solution.py:67
  51.8 0.0 copy-done.7
  51.8 0.0 copy-start.5
  51.8 0.1 convert_reduce_fusion
  51.9 0.0 copy-done.2
  51.9 2.7 reshape.107
  54.6 0.3 fusion.41
  55.0 47.1 %all-to-all-done = bf16[16,2,32,2048]{3,2,1,0:T(8,128)(2,1)} async-done(((bf16[16,2,32,2048]{3,2,1,0:T(8,128)(2,1)}), bf16[16,2,32,2048]{3,2,1,0:T(8,128)(2,1)}, u32[]{:S(2)}, u32[]{:S(2)}) %all-to-all-start) | async-done | bytes 4194336 | tf_op jit(solution)/shard_map/all_to_all | solution.py:67
  102.0 3.4 %bitcast_convert_fusion = f32[4,4,2,32,2048]{4,3,2,1,0:T(8,128)S(1)} fusion(bf16[16,2,32,2048]{3,2,1,0:T(8,128)(2,1)} %all-to-all-done), kind=kLoop, calls=%fused_computation.121 | loop fusion | flops 2097152 | bytes 12582912 | tf_op jit(solution)/shard_map/convert_element_type | solution.py:68
  105.5 3.0 %multiply_reduce_fusion = (f32[2,32]{1,0:T(2,128)S(1)}, f32[4,1,2,32,2048]{4,3,2,1,0:T(8,128)S(1)}, bf16[4,2,32,2048]{3,2,1,0:T(8,128)(2,1)}) fusion(f32[2,32,4,2048]{3,2,1,0:T(4,128)S(1)} %copy-done.4, f32[2,32]{1,0:T(2,128)S(1)} %add_rsqrt_fusion, f32[4,2048]{1,0:T(4,128)S(1)} %reshape.106, f32[4,4,2,32,2048]{4,3,2,1,0:T(8,128)S(1)} %bitcast_convert_fusion), kind=kLoop, calls=%fused_computation.78 | loop fusion | flops 4718528 | bytes 13664768 | tf_op jit(solution)/shard_map/reduce_sum | solution.py:76
  108.4 5.9 %all-to-all-start.3 = ((bf16[4,2,32,2048]{3,2,1,0:T(8,128)(2,1)}), bf16[4,2,32,2048]{3,2,1,0:T(8,128)(2,1)}, u32[]{:S(2)}, u32[]{:S(2)}) async-start(bf16[4,2,32,2048]{3,2,1,0:T(8,128)(2,1)} %get-tuple-element.20), calls=%async_computation.3 | async-start | bytes 2097152 | tf_op jit(solution)/shard_map/all_to_all | solution.py:81
  114.3 2.7 copy.102
  117.0 3.6 %reshape.101 = f32[1,2,32,8192]{3,2,1,0:T(8,128)} reshape(f32[2,32,4,2048]{3,2,1,0:T(4,128)} %copy.102) | data formatting | bytes 4194304 | tf_op jit(solution)/shard_map/reshape | solution.py:72
  120.6 0.0 copy-done.5
  120.6 3.1 %multiply_convert_fusion.1 = bf16[1,2,32,8192]{3,2,1,0:T(8,128)(2,1)} fusion(f32[1,2,32,8192]{3,2,1,0:T(8,128)} %reshape.101, bf16[1,2,32,8192]{3,2,1,0:T(8,128)(2,1)S(1)} %copy-done.2, f32[2,32]{1,0:T(2,128)S(1)} %broadcast_multiply_fusion, f32[8192]{0:T(1024)S(1)} %bitcast.151, f32[2,32]{1,0:T(2,128)S(1)} %add_rsqrt_fusion), kind=kLoop, calls=%fused_computation.77 | loop fusion | flops 3670016 | bytes 4227584 | tf_op jit(solution)/shard_map/convert_element_type | solution.py:32
  123.7 9.2 %copy.105 = bf16[1,2,32,8192]{2,1,0,3:T(2,128)(2,1)} copy(bf16[1,2,32,8192]{3,2,1,0:T(8,128)(2,1)} %multiply_convert_fusion.1) | data formatting | bytes 2097152 | tf_op jit(solution)/shard_map/convert_element_type | solution.py:32
  132.8 9.9 %reshape.147 = bf16[16,2,16384]{2,1,0:T(2,128)(2,1)} reshape(bf16[8192,1,2,32]{3,2,1,0:T(2,128)(2,1)} %bitcast.143) | data formatting | bytes 2097152
  142.8 0.0 all-to-all-done.3
  142.8 7.2 %all-to-all-start.1 = ((bf16[16,2,16384]{2,1,0:T(2,128)(2,1)}), bf16[16,2,16384]{2,1,0:T(2,128)(2,1)}, u32[]{:S(2)}, u32[]{:S(2)}) async-start(bf16[16,2,16384]{2,1,0:T(2,128)(2,1)} %reshape.147), calls=%async_computation.1 | async-start | bytes 2097152 | tf_op jit(solution)/shard_map/all_to_all | solution.py:31
  150.0 0.2 all-gather.7.cloned.1.call-start
  150.2 0.5 all-gather.7.cloned.1.call-update
  150.7 27.2 %all-to-all-done.1 = bf16[16,2,16384]{2,1,0:T(2,128)(2,1)} async-done(((bf16[16,2,16384]{2,1,0:T(2,128)(2,1)}), bf16[16,2,16384]{2,1,0:T(2,128)(2,1)}, u32[]{:S(2)}, u32[]{:S(2)}) %all-to-all-start.1) | async-done | bytes 1048608 | tf_op jit(solution)/shard_map/all_to_all | solution.py:31
  177.9 10.0 %reshape.148 = bf16[8192,1,2,32]{3,2,1,0:T(2,128)(2,1)} reshape(bf16[16,2,16384]{2,1,0:T(2,128)(2,1)} %all-to-all-done.1) | data formatting | bytes 2097152
  187.9 9.0 %copy.106 = bf16[1,2,32,8192]{3,2,1,0:T(8,128)(2,1)} copy(bf16[1,2,32,8192]{2,1,0,3:T(2,128)(2,1)} %bitcast.144) | data formatting | bytes 2097152 | tf_op jit(solution)/shard_map/all_to_all | solution.py:31
  196.9 1.6 copy.154
  198.6 1.8 fusion.61
  200.6 0.1 copy.124
  200.8 0.1 copy.122
  200.9 0.8 copy.123
  201.7 0.8 copy.126
  202.4 0.8 copy.128
  203.2 0.8 copy.130
  204.0 0.8 copy.134
  204.7 0.8 copy.132
  205.5 0.8 copy.125
  206.3 0.7 copy.127
  207.0 0.8 copy.129
  207.8 0.8 copy.131
  208.5 0.8 copy.133
  209.3 0.7 reshape.112
  210.1 0.2 fusion.53
  210.3 0.7 stack_broadcast_in_dim.3
  211.0 7.5 %stack.3 = bf16[16,2,32,512]{3,0,2,1:T(8,128)(2,1)} concatenate(bf16[1,2,32,512]{3,0,2,1:T(2,128)(2,1)S(1)} %fusion.53, bf16[1,2,32,512]{3,0,2,1:T(2,128)(2,1)S(1)} %copy.122, bf16[1,2,32,512]{3,0,2,1:T(2,128)(2,1)} %copy.123, bf16[1,2,32,512]{3,0,2,1:T(2,128)(2,1)S(1)} %copy.124, bf16[1,2,32,512]{3,0,2,1:T(2,128)(2,1)} %copy.125, bf16[1,2,32,512]{3,0,2,1:T(2,128)(2,1)} %copy.126, ...), dimensions={0} | concatenate | bytes 2097152 | tf_op jit(solution)/shard_map/stack | solution.py:39
  218.5 2.8 copy.135
  221.3 4.6 %all-to-all-start.2 = ((bf16[16,2,32,512]{3,2,1,0:T(8,128)(2,1)}), bf16[16,2,32,512]{3,2,1,0:T(8,128)(2,1)}, u32[]{:S(2)}, u32[]{:S(2)}) async-start(bf16[16,2,32,512]{3,2,1,0:T(8,128)(2,1)} %copy.135), calls=%async_computation.2 | async-start | bytes 2097152 | tf_op jit(solution)/shard_map/all_to_all | solution.py:40
  227.2 1.6 copy.153
  228.7 23.9 %all-to-all-done.2 = bf16[16,2,32,512]{3,2,1,0:T(8,128)(2,1)} async-done(((bf16[16,2,32,512]{3,2,1,0:T(8,128)(2,1)}), bf16[16,2,32,512]{3,2,1,0:T(8,128)(2,1)}, u32[]{:S(2)}, u32[]{:S(2)}) %all-to-all-start.2) | async-done | bytes 1048608 | tf_op jit(solution)/shard_map/all_to_all | solution.py:40
  252.6 1.5 convert_bitcast_fusion
  254.1 0.0 copy-start.6
  254.1 2.5 copy.136
  256.7 2.9 %reshape.110 = f32[2,32,8192]{2,1,0:T(8,128)} reshape(f32[1,2,32,16,512]{4,3,2,1,0:T(8,128)} %copy.136) | data formatting | bytes 4194304 | tf_op jit(solution)/shard_map/convert_element_type | solution.py:41
  259.6 0.0 copy-done.6
  259.6 3.5 %fusion.49 = bf16[1,2,32,8192]{3,2,1,0:T(8,128)(2,1)} fusion(f32[2,32,8192]{2,1,0:T(8,128)} %reshape.110, bf16[1,2,32,8192]{3,2,1,0:T(8,128)(2,1)S(1)} %copy-done.2, f32[2,32,8192]{2,1,0:T(8,128)S(1)} %bitcast.146, bf16[2,32,8192]{2,1,0:T(8,128)(2,1)} %param.11, f32[2,32]{1,0:T(2,128)S(1)} %broadcast_multiply_fusion, f32[8192]{0:T(1024)S(1)} %bitcast.152, ...), kind=kLoop, calls=%fused_computation.80 | loop fusion | flops 5242880 | bytes 7373312 | tf_op jit(solution)/shard_map/broadcast_in_dim | solution.py:94
  263.1 4.9 %convolution_bitcast_fusion = f32[4,2048,512]{2,1,0:T(8,128)S(1)} fusion(bf16[4,4,2,32,2048]{4,3,2,1,0:T(8,128)(2,1)} %bitcast.154, bf16[2,4,4,32,512]{4,3,2,1,0:T(8,128)(2,1)} %bitcast.155), kind=kOutput, calls=%fused_computation | convolution fusion | flops 2147483648 | bytes 22020096 | tf_op jit(solution)/shard_map/tpmid,mptik->pdk/dot_general | solution.py:84
  268.0 10.4 %fusion.39 = (bf16[2048,512]{1,0:T(8,128)(2,1)S(1)}, bf16[2048,512]{1,0:T(8,128)(2,1)S(1)}, bf16[2048,512]{1,0:T(8,128)(2,1)S(1)}, bf16[2048,512]{1,0:T(8,128)(2,1)S(1)}) fusion(f32[4,2048,512]{2,1,0:T(8,128)S(1)} %convolution_bitcast_fusion, s32[]{:T(128)S(6)} %mul.216, s32[]{:T(128)} %bitcast.37, s32[]{:T(128)} %bitcast.36, s32[2048]{0:T(1024)S(1)} %multiply_add_fusion), kind=kLoop, calls=%fused_computation.59 | loop fusion | flops 75497472 | bytes 25174028 | tf_op jit(solution)/shard_map/convert_element_type | solution.py:25
  278.4 0.0 copy-start.1
  278.4 3.2 %add_bitcast_fusion = f32[1,2048,512]{2,1,0:T(8,128)} fusion(bf16[2048,512]{1,0:T(8,128)(2,1)S(1)} %get-tuple-element.17, bf16[2048,512]{1,0:T(8,128)(2,1)S(1)} %get-tuple-element.18, bf16[2048,512]{1,0:T(8,128)(2,1)S(1)} %get-tuple-element.19, bf16[2048,512]{1,0:T(8,128)(2,1)S(1)} %get-tuple-element.16), kind=kLoop, calls=%fused_computation.54 | loop fusion | flops 7340032 | bytes 12582912 | tf_op jit(solution)/shard_map/broadcast_in_dim | solution.py:94
  (21 shorter events, 0.3 us)
Async XLA Ops:
  7.2 31.0 %copy-start = (bf16[1,2048,512]{2,1,0:T(8,128)(2,1)S(1)}, bf16[1,2048,512]{2,1,0:T(8,128)(2,1)}, u32[]{:S(2)}) copy-start(bf16[1,2048,512]{2,1,0:T(8,128)(2,1)} %param.9) | copy-start | bytes 6291460
  7.2 31.0 %all-gather.5.cloned.1.call-start = ((), (), s32[]{:S(2)}) async-start(), calls=%async_computation.4 | async-start | bytes 1310720 | tf_op jit(solution)/shard_map/all_gather | solution.py:62
  44.1 7.6 %copy-start.7 = (bf16[1,8192]{1,0:T(2,128)(2,1)S(1)}, bf16[1,8192]{1,0:T(2,128)(2,1)}, u32[]{:S(2)}) copy-start(bf16[1,8192]{1,0:T(2,128)(2,1)} %param.10) | copy-start | bytes 49156
  44.1 7.8 %copy-start.2 = (bf16[1,2,32,8192]{3,2,1,0:T(8,128)(2,1)S(1)}, bf16[1,2,32,8192]{3,2,1,0:T(8,128)(2,1)}, u32[]{:S(2)}) copy-start(bf16[1,2,32,8192]{3,2,1,0:T(8,128)(2,1)} %param.7) | copy-start | bytes 3145732
  44.1 57.9 %all-to-all-start = ((bf16[16,2,32,2048]{3,2,1,0:T(8,128)(2,1)}), bf16[16,2,32,2048]{3,2,1,0:T(8,128)(2,1)}, u32[]{:S(2)}, u32[]{:S(2)}) async-start(bf16[16,2,32,2048]{3,2,1,0:T(8,128)(2,1)} %bitcast.145), calls=%async_computation | async-start | bytes 8388608 | tf_op jit(solution)/shard_map/all_to_all | solution.py:67
  51.8 68.8 %copy-start.5 = (f32[1,8192]{1,0:T(1,128)}, f32[1,8192]{1,0:T(1,128)S(1)}, u32[]{:S(2)}) copy-start(f32[1,8192]{1,0:T(1,128)S(1)} %convert_element_type.151) | copy-start | bytes 98308
  102.0 3.4 %copy-start.4 = (f32[2,32,4,2048]{3,2,1,0:T(4,128)S(1)}, f32[2,32,4,2048]{3,2,1,0:T(4,128)}, u32[]{:S(2)}) copy-start(f32[2,32,4,2048]{3,2,1,0:T(4,128)} %reshape.107) | copy-start | bytes 6291460
  108.4 34.3 %all-to-all-start.3 = ((bf16[4,2,32,2048]{3,2,1,0:T(8,128)(2,1)}), bf16[4,2,32,2048]{3,2,1,0:T(8,128)(2,1)}, u32[]{:S(2)}, u32[]{:S(2)}) async-start(bf16[4,2,32,2048]{3,2,1,0:T(8,128)(2,1)} %get-tuple-element.20), calls=%async_computation.3 | async-start | bytes 2097152 | tf_op jit(solution)/shard_map/all_to_all | solution.py:81
  142.8 35.1 %all-to-all-start.1 = ((bf16[16,2,16384]{2,1,0:T(2,128)(2,1)}), bf16[16,2,16384]{2,1,0:T(2,128)(2,1)}, u32[]{:S(2)}, u32[]{:S(2)}) async-start(bf16[16,2,16384]{2,1,0:T(2,128)(2,1)} %reshape.147), calls=%async_computation.1 | async-start | bytes 2097152 | tf_op jit(solution)/shard_map/all_to_all | solution.py:31
  150.0 113.2 %all-gather.7.cloned.1.call-start = ((), (), s32[]{:S(2)}) async-start(), calls=%async_computation.5 | async-start | bytes 5242880 | tf_op jit(solution)/shard_map/all_gather | solution.py:82
  221.3 31.3 %all-to-all-start.2 = ((bf16[16,2,32,512]{3,2,1,0:T(8,128)(2,1)}), bf16[16,2,32,512]{3,2,1,0:T(8,128)(2,1)}, u32[]{:S(2)}, u32[]{:S(2)}) async-start(bf16[16,2,32,512]{3,2,1,0:T(8,128)(2,1)} %copy.135), calls=%async_computation.2 | async-start | bytes 2097152 | tf_op jit(solution)/shard_map/all_to_all | solution.py:40
  254.1 5.5 %copy-start.6 = (f32[1,8192]{1,0:T(1,128)S(1)}, f32[1,8192]{1,0:T(1,128)}, u32[]{:S(2)}) copy-start(f32[1,8192]{1,0:T(1,128)} %copy-done.5) | copy-start | bytes 98308
  256.7 2.9 %copy-start.3 = (f32[4,2,4,8,2048]{4,3,0,2,1:T(8,128)S(1)}, f32[4,2,4,8,2048]{4,3,0,2,1:T(8,128)}, u32[]{:S(2)}) copy-start(f32[4,2,4,8,2048]{4,3,0,2,1:T(8,128)} %copy.153) | copy-start | bytes 6291460
  278.4 3.2 %copy-start.1 = (bf16[1,2048,512]{2,1,0:T(8,128)(2,1)S(1)}, bf16[1,2048,512]{2,1,0:T(8,128)(2,1)}, u32[]{:S(2)}) copy-start(bf16[1,2048,512]{2,1,0:T(8,128)(2,1)} %param.9) | copy-start | bytes 6291460
Sparse Core Ops, SparseCore 0:
  9.8 28.3 all-gather.4
  152.6 46.6 all-gather.6
where the time goes:
time: 290 us; the launch traced here: 288 us
  waiting for transfers between devices  130 us (45%)
  local copies, waits for them, and re-layouts  80.4 us (28%)
  other arithmetic  28.9 us (10%)
  starting transfers between devices  25.5 us (9%)
  between operations  15.6 us (5%)
  matrix products  8.46 us (3%)
    all_to_all x1, waiting for transfers between devices, shards(): got = lax.all_to_all(part, ('dp', 'tensor'), 0, 0, tiled=True)  47.1 us
    all_gather x1, waiting for transfers between devices, shards(): cotan_all = lax.all_gather(cotan, 'dp', axis=1, tiled=True)  30.3 us
    all_to_all x1, waiting for transfers between devices, later_sum(): lax.all_to_all(branch_path.astype(jnp.bfloat16)[None], 'section', 3, 0, t...  27.2 us
    all_to_all x1, waiting for transfers between devices, later_sum(): back = lax.all_to_all(stacked, 'section', 0, 3, tiled=True)  23.9 us
    unnamed x20, local copies, waits for them, and re-layouts  21.6 us
    another operation x3, local copies, waits for them, and re-layouts, later_sum(): stacked = jnp.stack(outs).astype(jnp.bfloat16)  11 us
    convert_element_type x1, other arithmetic, dither(): moved.astype(jnp.bfloat16)  10.4 us
    another operation x14, local copies, waits for them, and re-layouts  9.33 us
  transfers between devices with their start and end apart: 6, of which 4 were waited for; matrix products, arithmetic and copies ran while one was open for 30% of the time, Pallas kernels for 0%

commit v1 on v0

--- a/solution.py
+++ b/solution.py
@@ -2,6 +2,19 @@
 import jax.numpy as jnp
 from jax import lax
 from jax.sharding import PartitionSpec as P
+
+
+def collect(value, axis, dim):
+    ways = lax.axis_size(axis)
+    up = [(d, (d + 1) % ways) for d in range(ways)]
+    down = [(d, (d - 1) % ways) for d in range(ways)]
+    earlier, later = ([value], [value])
+    for _ in range(ways // 2):
+        earlier.append(lax.ppermute(earlier[-1], axis, up))
+    for _ in range((ways - 1) // 2):
+        later.append(lax.ppermute(later[-1], axis, down))
+    line = jnp.concatenate([*earlier[::-1], *later[1:]], axis=dim)
+    return jnp.roll(line, (lax.axis_index(axis) - ways // 2) * value.shape[dim], axis=dim)
 
 
 def mix_bits(salt, counter, layer, group, index):
@@ -59,7 +72,7 @@
     centered_input = input_float * inverse_scale
     gain_float = norm_gain[0].astype(jnp.float32)
     normed_values = (centered_input * gain_float).astype(jnp.bfloat16)
-    cotan_all = lax.all_gather(cotan, "dp", axis=1, tiled=True)
+    cotan_all = collect(cotan, "dp", 1)
     part = jnp.einsum("mtk,dk->mtd", cotan_all, weight, preferred_element_type=jnp.float32).astype(
         jnp.bfloat16
     )

time: 290 us -> 279 us (0.962)
  waiting for transfers between devices: 130 us -> 111 us
  starting transfers between devices: 25.5 us -> 31.6 us
    all_gather x1 -> x0, waiting for transfers between devices: 30.3 us -> none  [shards(): cotan_all = lax.all_gather(cotan, 'dp', axis=1, tiled=True)]
    ppermute x0 -> x3, waiting for transfers between devices: none -> 12.3 us  [the longest x2 11.7 us: collect(): earlier.append(lax.ppermute(earlier[-1], axis, up))]
    ppermute x0 -> x3, starting transfers between devices: none -> 3.68 us  [the longest x2 3.23 us: collect(): earlier.append(lax.ppermute(earlier[-1], axis, up))]
    unnamed x20 -> x29, local copies, waits for them, and re-layouts: 21.6 us -> 23.6 us
  transfers between devices with their start and end apart: 6 -> 8, of which waited for: 4 -> 6; matrix products, arithmetic and copies ran while one was open for 30% -> 32% of each run, Pallas kernels for 0% -> 0%
where the time goes in v1:
time: 279 us; the launch traced here: 277 us
  waiting for transfers between devices  111 us (40%)
  local copies, waits for them, and re-layouts  82.3 us (29%)
  starting transfers between devices  31.6 us (11%)
  other arithmetic  28.9 us (10%)
  between operations  15.7 us (6%)
  matrix products  7.24 us (3%)
    all_to_all x1, waiting for transfers between devices, shards(): got = lax.all_to_all(part, ('dp', 'tensor'), 0, 0, tiled=True)  47.1 us
    all_to_all x1, waiting for transfers between devices, later_sum(): lax.all_to_all(branch_path.astype(jnp.bfloat16)[None], 'section', 3, 0, t...  27.2 us
    all_to_all x1, waiting for transfers between devices, later_sum(): back = lax.all_to_all(stacked, 'section', 0, 3, tiled=True)  23.9 us
    unnamed x29, local copies, waits for them, and re-layouts  23.6 us
    ppermute x2, waiting for transfers between devices, collect(): earlier.append(lax.ppermute(earlier[-1], axis, up))  11.7 us
    another operation x3, local copies, waits for them, and re-layouts, later_sum(): stacked = jnp.stack(outs).astype(jnp.bfloat16)  11 us
    convert_element_type x1, other arithmetic, dither(): moved.astype(jnp.bfloat16)  10.4 us
    another operation x14, local copies, waits for them, and re-layouts  9.21 us
  transfers between devices with their start and end apart: 8, of which 6 were waited for; matrix products, arithmetic and copies ran while one was open for 32% of the time, Pallas kernels for 0%

profile of v1, /device:TPU:8, one launch (start us, length us, event | category | flops | bytes accessed | tf_op | source)
XLA Modules:
  0.0 276.7 jit_solution(3206488395415982483)
XLA Ops:
  7.2 0.0 copy-start
  7.2 1.7 collective-permute-start
  8.8 6.7 %collective-permute-done = bf16[2,128,512]{2,1,0:T(8,128)(2,1)S(1)} collective-permute-done((bf16[2,128,512]{2,1,0:T(8,128)(2,1)}, bf16[2,128,512]{2,1,0:T(8,128)(2,1)S(1)}, u32[]{:S(2)}, u32[]{:S(2)}) %collective-permute-start) | collective-permute-done | bytes 262176 | tf_op jit(solution)/shard_map/ppermute | solution.py:13
  15.5 1.6 collective-permute-start.1
  17.1 0.4 collective-permute-start.2
  17.5 5.0 %collective-permute-done.1 = bf16[2,128,512]{2,1,0:T(8,128)(2,1)S(1)} collective-permute-done((bf16[2,128,512]{2,1,0:T(8,128)(2,1)S(1)}, bf16[2,128,512]{2,1,0:T(8,128)(2,1)S(1)}, u32[]{:S(2)}, u32[]{:S(2)}) %collective-permute-start.1) | collective-permute-done | bytes 262176 | tf_op jit(solution)/shard_map/ppermute | solution.py:13
  22.6 1.0 constant_dynamic-update-slice_fusion.5
  23.6 0.6 collective-permute-done.2
  24.3 1.0 constant_dynamic-update-slice_fusion.1
  25.3 0.1 constant_dynamic-slice_fusion
  25.4 2.4 convolution_convert_fusion
  27.8 2.3 copy.236
  30.1 8.5 %all-to-all-start = ((bf16[16,2,32,2048]{3,2,1,0:T(8,128)(2,1)}), bf16[16,2,32,2048]{3,2,1,0:T(8,128)(2,1)}, u32[]{:S(2)}, u32[]{:S(2)}) async-start(bf16[16,2,32,2048]{3,2,1,0:T(8,128)(2,1)} %bitcast.146), calls=%async_computation | async-start | bytes 8388608 | tf_op jit(solution)/shard_map/all_to_all | solution.py:80
  38.7 0.1 convert_reduce_fusion
  38.8 0.0 copy-done.2
  38.8 2.7 reshape.107
  41.5 0.3 fusion.41
  41.8 47.1 %all-to-all-done = bf16[16,2,32,2048]{3,2,1,0:T(8,128)(2,1)} async-done(((bf16[16,2,32,2048]{3,2,1,0:T(8,128)(2,1)}), bf16[16,2,32,2048]{3,2,1,0:T(8,128)(2,1)}, u32[]{:S(2)}, u32[]{:S(2)}) %all-to-all-start) | async-done | bytes 4194336 | tf_op jit(solution)/shard_map/all_to_all | solution.py:80
  88.9 3.4 %bitcast_convert_fusion = f32[4,4,2,32,2048]{4,3,2,1,0:T(8,128)S(1)} fusion(bf16[16,2,32,2048]{3,2,1,0:T(8,128)(2,1)} %all-to-all-done), kind=kLoop, calls=%fused_computation.129 | loop fusion | flops 2097152 | bytes 12582912 | tf_op jit(solution)/shard_map/convert_element_type | solution.py:81
  92.3 3.0 %multiply_reduce_fusion = (f32[2,32]{1,0:T(2,128)S(1)}, f32[4,1,2,32,2048]{4,3,2,1,0:T(8,128)S(1)}, bf16[4,2,32,2048]{3,2,1,0:T(8,128)(2,1)}) fusion(f32[2,32,4,2048]{3,2,1,0:T(4,128)S(1)} %copy-done.4, f32[2,32]{1,0:T(2,128)S(1)} %add_rsqrt_fusion, f32[4,2048]{1,0:T(4,128)S(1)} %reshape.106, f32[4,4,2,32,2048]{4,3,2,1,0:T(8,128)S(1)} %bitcast_convert_fusion), kind=kLoop, calls=%fused_computation.78 | loop fusion | flops 4718528 | bytes 13664768 | tf_op jit(solution)/shard_map/reduce_sum | solution.py:89
  95.3 5.9 %all-to-all-start.3 = ((bf16[4,2,32,2048]{3,2,1,0:T(8,128)(2,1)}), bf16[4,2,32,2048]{3,2,1,0:T(8,128)(2,1)}, u32[]{:S(2)}, u32[]{:S(2)}) async-start(bf16[4,2,32,2048]{3,2,1,0:T(8,128)(2,1)} %get-tuple-element.20), calls=%async_computation.3 | async-start | bytes 2097152 | tf_op jit(solution)/shard_map/all_to_all | solution.py:94
  101.2 2.7 copy.101
  103.8 3.6 %reshape.101 = f32[1,2,32,8192]{3,2,1,0:T(8,128)} reshape(f32[2,32,4,2048]{3,2,1,0:T(4,128)} %copy.101) | data formatting | bytes 4194304 | tf_op jit(solution)/shard_map/reshape | solution.py:85
  107.5 3.1 %multiply_convert_fusion.1 = bf16[1,2,32,8192]{3,2,1,0:T(8,128)(2,1)} fusion(f32[1,2,32,8192]{3,2,1,0:T(8,128)} %reshape.101, bf16[1,2,32,8192]{3,2,1,0:T(8,128)(2,1)S(1)} %copy-done.2, f32[2,32]{1,0:T(2,128)S(1)} %broadcast_multiply_fusion, f32[8192]{0:T(1024)S(1)} %bitcast.155, f32[2,32]{1,0:T(2,128)S(1)} %add_rsqrt_fusion), kind=kLoop, calls=%fused_computation.77 | loop fusion | flops 3670016 | bytes 4227584 | tf_op jit(solution)/shard_map/convert_element_type | solution.py:45
  110.6 9.2 %copy.104 = bf16[1,2,32,8192]{2,1,0,3:T(2,128)(2,1)} copy(bf16[1,2,32,8192]{3,2,1,0:T(8,128)(2,1)} %multiply_convert_fusion.1) | data formatting | bytes 2097152 | tf_op jit(solution)/shard_map/convert_element_type | solution.py:45
  119.7 9.9 %reshape.145 = bf16[16,2,16384]{2,1,0:T(2,128)(2,1)} reshape(bf16[8192,1,2,32]{3,2,1,0:T(2,128)(2,1)} %bitcast.144) | data formatting | bytes 2097152
  129.6 0.0 all-to-all-done.3
  129.6 8.6 %all-to-all-start.1 = ((bf16[16,2,16384]{2,1,0:T(2,128)(2,1)}), bf16[16,2,16384]{2,1,0:T(2,128)(2,1)}, u32[]{:S(2)}, u32[]{:S(2)}) async-start(bf16[16,2,16384]{2,1,0:T(2,128)(2,1)} %reshape.145), calls=%async_computation.1 | async-start | bytes 2097152 | tf_op jit(solution)/shard_map/all_to_all | solution.py:44
  138.3 0.3 all-gather.3.cloned.1.call-start
  138.6 0.5 all-gather.3.cloned.1.call-update
  139.0 27.2 %all-to-all-done.1 = bf16[16,2,16384]{2,1,0:T(2,128)(2,1)} async-done(((bf16[16,2,16384]{2,1,0:T(2,128)(2,1)}), bf16[16,2,16384]{2,1,0:T(2,128)(2,1)}, u32[]{:S(2)}, u32[]{:S(2)}) %all-to-all-start.1) | async-done | bytes 1048608 | tf_op jit(solution)/shard_map/all_to_all | solution.py:44
  166.3 10.0 %reshape.146 = bf16[8192,1,2,32]{3,2,1,0:T(2,128)(2,1)} reshape(bf16[16,2,16384]{2,1,0:T(2,128)(2,1)} %all-to-all-done.1) | data formatting | bytes 2097152
  176.3 9.0 %copy.105 = bf16[1,2,32,8192]{3,2,1,0:T(8,128)(2,1)} copy(bf16[1,2,32,8192]{2,1,0,3:T(2,128)(2,1)} %bitcast.145) | data formatting | bytes 2097152 | tf_op jit(solution)/shard_map/all_to_all | solution.py:44
  185.3 1.6 copy.153
  186.9 1.8 fusion.60
  189.0 0.1 copy.123
  189.1 0.1 copy.121
  189.3 0.8 copy.122
  190.0 0.8 copy.125
  190.8 0.8 copy.127
  191.5 0.7 copy.129
  192.3 0.8 copy.133
  193.0 0.8 copy.131
  193.8 0.8 copy.124
  194.5 0.8 copy.126
  195.3 0.8 copy.128
  196.0 0.8 copy.130
  196.8 0.8 copy.132
  197.6 0.7 reshape.112
  198.3 0.2 fusion.52
  198.5 0.7 stack_broadcast_in_dim.3
  199.2 7.5 %stack.3 = bf16[16,2,32,512]{3,0,2,1:T(8,128)(2,1)} concatenate(bf16[1,2,32,512]{3,0,2,1:T(2,128)(2,1)S(1)} %fusion.52, bf16[1,2,32,512]{3,0,2,1:T(2,128)(2,1)S(1)} %copy.121, bf16[1,2,32,512]{3,0,2,1:T(2,128)(2,1)} %copy.122, bf16[1,2,32,512]{3,0,2,1:T(2,128)(2,1)S(1)} %copy.123, bf16[1,2,32,512]{3,0,2,1:T(2,128)(2,1)} %copy.124, bf16[1,2,32,512]{3,0,2,1:T(2,128)(2,1)} %copy.125, ...), dimensions={0} | concatenate | bytes 2097152 | tf_op jit(solution)/shard_map/stack | solution.py:52
  206.7 2.8 %copy.134 = bf16[16,2,32,512]{3,2,1,0:T(8,128)(2,1)} copy(bf16[16,2,32,512]{3,0,2,1:T(8,128)(2,1)} %stack.3) | data formatting | bytes 2097152 | tf_op jit(solution)/shard_map/stack | solution.py:52
  209.5 4.6 %all-to-all-start.2 = ((bf16[16,2,32,512]{3,2,1,0:T(8,128)(2,1)}), bf16[16,2,32,512]{3,2,1,0:T(8,128)(2,1)}, u32[]{:S(2)}, u32[]{:S(2)}) async-start(bf16[16,2,32,512]{3,2,1,0:T(8,128)(2,1)} %copy.134), calls=%async_computation.2 | async-start | bytes 2097152 | tf_op jit(solution)/shard_map/all_to_all | solution.py:53
  215.4 1.6 copy.152
  217.0 23.9 %all-to-all-done.2 = bf16[16,2,32,512]{3,2,1,0:T(8,128)(2,1)} async-done(((bf16[16,2,32,512]{3,2,1,0:T(8,128)(2,1)}), bf16[16,2,32,512]{3,2,1,0:T(8,128)(2,1)}, u32[]{:S(2)}, u32[]{:S(2)}) %all-to-all-start.2) | async-done | bytes 1048608 | tf_op jit(solution)/shard_map/all_to_all | solution.py:53
  240.8 1.5 convert_bitcast_fusion
  242.4 2.5 copy.135
  244.9 2.9 %reshape.110 = f32[2,32,8192]{2,1,0:T(8,128)} reshape(f32[1,2,32,16,512]{4,3,2,1,0:T(8,128)} %copy.135) | data formatting | bytes 4194304 | tf_op jit(solution)/shard_map/convert_element_type | solution.py:54
  247.8 3.5 %fusion.49 = bf16[1,2,32,8192]{3,2,1,0:T(8,128)(2,1)} fusion(f32[2,32,8192]{2,1,0:T(8,128)} %reshape.110, bf16[1,2,32,8192]{3,2,1,0:T(8,128)(2,1)S(1)} %copy-done.2, f32[2,32,8192]{2,1,0:T(8,128)S(1)} %bitcast.147, bf16[2,32,8192]{2,1,0:T(8,128)(2,1)} %param.11, f32[2,32]{1,0:T(2,128)S(1)} %broadcast_multiply_fusion, f32[8192]{0:T(1024)S(1)} %bitcast.156, ...), kind=kLoop, calls=%fused_computation.80 | loop fusion | flops 5242880 | bytes 7373312 | tf_op jit(solution)/shard_map/broadcast_in_dim | solution.py:107
  251.4 4.9 %convolution_bitcast_fusion = f32[4,2048,512]{2,1,0:T(8,128)S(1)} fusion(bf16[4,4,2,32,2048]{4,3,2,1,0:T(8,128)(2,1)} %bitcast.158, bf16[2,4,4,32,512]{4,3,2,1,0:T(8,128)(2,1)} %bitcast.152), kind=kOutput, calls=%fused_computation | convolution fusion | flops 2147483648 | bytes 22020096 | tf_op jit(solution)/shard_map/tpmid,mptik->pdk/dot_general | solution.py:97
  256.2 10.4 %fusion.39 = (bf16[2048,512]{1,0:T(8,128)(2,1)S(1)}, bf16[2048,512]{1,0:T(8,128)(2,1)S(1)}, bf16[2048,512]{1,0:T(8,128)(2,1)S(1)}, bf16[2048,512]{1,0:T(8,128)(2,1)S(1)}) fusion(f32[4,2048,512]{2,1,0:T(8,128)S(1)} %convolution_bitcast_fusion, s32[]{:T(128)S(6)} %mul.220, s32[]{:T(128)} %bitcast.37, s32[]{:T(128)} %bitcast.36, s32[2048]{0:T(1024)S(1)} %multiply_add_fusion), kind=kLoop, calls=%fused_computation.59 | loop fusion | flops 75497472 | bytes 25174028 | tf_op jit(solution)/shard_map/convert_element_type | solution.py:38
  266.6 0.0 copy-start.1
  266.7 3.2 %add_bitcast_fusion = f32[1,2048,512]{2,1,0:T(8,128)} fusion(bf16[2048,512]{1,0:T(8,128)(2,1)S(1)} %get-tuple-element.17, bf16[2048,512]{1,0:T(8,128)(2,1)S(1)} %get-tuple-element.18, bf16[2048,512]{1,0:T(8,128)(2,1)S(1)} %get-tuple-element.19, bf16[2048,512]{1,0:T(8,128)(2,1)S(1)} %get-tuple-element.16), kind=kLoop, calls=%fused_computation.54 | loop fusion | flops 7340032 | bytes 12582912 | tf_op jit(solution)/shard_map/broadcast_in_dim | solution.py:107
  (35 shorter events, 0.4 us)
Async XLA Ops:
  7.2 18.2 %copy-start = (bf16[1,2048,512]{2,1,0:T(8,128)(2,1)S(1)}, bf16[1,2048,512]{2,1,0:T(8,128)(2,1)}, u32[]{:S(2)}) copy-start(bf16[1,2048,512]{2,1,0:T(8,128)(2,1)} %param.9) | copy-start | bytes 6291460
  7.2 8.3 %collective-permute-start = (bf16[2,128,512]{2,1,0:T(8,128)(2,1)}, bf16[2,128,512]{2,1,0:T(8,128)(2,1)S(1)}, u32[]{:S(2)}, u32[]{:S(2)}) collective-permute-start(bf16[2,128,512]{2,1,0:T(8,128)(2,1)} %bitcast.153), channel_id=1, source_target_pairs={{0,64},{64,128},{128,192},{192,0},{1,65},{65,129},{129,193},{193,1... | collective-permute-start | bytes 786440 | tf_op jit(solution)/shard_map/ppermute | solution.py:13
  15.5 7.0 %collective-permute-start.1 = (bf16[2,128,512]{2,1,0:T(8,128)(2,1)S(1)}, bf16[2,128,512]{2,1,0:T(8,128)(2,1)S(1)}, u32[]{:S(2)}, u32[]{:S(2)}) collective-permute-start(bf16[2,128,512]{2,1,0:T(8,128)(2,1)S(1)} %collective-permute-done), channel_id=1, source_target_pairs={{0,64},{64,128},{128,192},{192,0},{1,65},{65,129},{129,193},{193,1... | collective-permute-start | bytes 786440 | tf_op jit(solution)/shard_map/ppermute | solution.py:13
  17.1 7.1 %collective-permute-start.2 = (bf16[2,128,512]{2,1,0:T(8,128)(2,1)}, bf16[2,128,512]{2,1,0:T(8,128)(2,1)S(1)}, u32[]{:S(2)}, u32[]{:S(2)}) collective-permute-start(bf16[2,128,512]{2,1,0:T(8,128)(2,1)} %bitcast.154), channel_id=1, source_target_pairs={{0,192},{64,0},{128,64},{192,128},{1,193},{65,1},{129,65},{193,129... | collective-permute-start | bytes 786440 | tf_op jit(solution)/shard_map/ppermute | solution.py:15
  25.4 2.4 copy-start.5
  30.1 8.6 %copy-start.8 = (bf16[1,8192]{1,0:T(2,128)(2,1)S(1)}, bf16[1,8192]{1,0:T(2,128)(2,1)}, u32[]{:S(2)}) copy-start(bf16[1,8192]{1,0:T(2,128)(2,1)} %param.10) | copy-start | bytes 49156
  30.1 8.7 %copy-start.2 = (bf16[1,2,32,8192]{3,2,1,0:T(8,128)(2,1)S(1)}, bf16[1,2,32,8192]{3,2,1,0:T(8,128)(2,1)}, u32[]{:S(2)}) copy-start(bf16[1,2,32,8192]{3,2,1,0:T(8,128)(2,1)} %param.7) | copy-start | bytes 3145732
  30.1 58.8 %all-to-all-start = ((bf16[16,2,32,2048]{3,2,1,0:T(8,128)(2,1)}), bf16[16,2,32,2048]{3,2,1,0:T(8,128)(2,1)}, u32[]{:S(2)}, u32[]{:S(2)}) async-start(bf16[16,2,32,2048]{3,2,1,0:T(8,128)(2,1)} %bitcast.146), calls=%async_computation | async-start | bytes 8388608 | tf_op jit(solution)/shard_map/all_to_all | solution.py:80
  38.7 68.8 %copy-start.6 = (f32[1,8192]{1,0:T(1,128)}, f32[1,8192]{1,0:T(1,128)S(1)}, u32[]{:S(2)}) copy-start(f32[1,8192]{1,0:T(1,128)S(1)} %convert_element_type.151) | copy-start | bytes 98308
  88.9 3.4 %copy-start.4 = (f32[2,32,4,2048]{3,2,1,0:T(4,128)S(1)}, f32[2,32,4,2048]{3,2,1,0:T(4,128)}, u32[]{:S(2)}) copy-start(f32[2,32,4,2048]{3,2,1,0:T(4,128)} %reshape.107) | copy-start | bytes 6291460
  95.3 34.3 %all-to-all-start.3 = ((bf16[4,2,32,2048]{3,2,1,0:T(8,128)(2,1)}), bf16[4,2,32,2048]{3,2,1,0:T(8,128)(2,1)}, u32[]{:S(2)}, u32[]{:S(2)}) async-start(bf16[4,2,32,2048]{3,2,1,0:T(8,128)(2,1)} %get-tuple-element.20), calls=%async_computation.3 | async-start | bytes 2097152 | tf_op jit(solution)/shard_map/all_to_all | solution.py:94
  129.6 36.6 %all-to-all-start.1 = ((bf16[16,2,16384]{2,1,0:T(2,128)(2,1)}), bf16[16,2,16384]{2,1,0:T(2,128)(2,1)}, u32[]{:S(2)}, u32[]{:S(2)}) async-start(bf16[16,2,16384]{2,1,0:T(2,128)(2,1)} %reshape.145), calls=%async_computation.1 | async-start | bytes 2097152 | tf_op jit(solution)/shard_map/all_to_all | solution.py:44
  138.3 113.1 %all-gather.3.cloned.1.call-start = ((), (), s32[]{:S(2)}) async-start(), calls=%async_computation.4 | async-start | bytes 5242880 | tf_op jit(solution)/shard_map/all_gather | solution.py:95
  209.5 31.3 %all-to-all-start.2 = ((bf16[16,2,32,512]{3,2,1,0:T(8,128)(2,1)}), bf16[16,2,32,512]{3,2,1,0:T(8,128)(2,1)}, u32[]{:S(2)}, u32[]{:S(2)}) async-start(bf16[16,2,32,512]{3,2,1,0:T(8,128)(2,1)} %copy.134), calls=%async_computation.2 | async-start | bytes 2097152 | tf_op jit(solution)/shard_map/all_to_all | solution.py:53
  242.3 5.5 %copy-start.7 = (f32[1,8192]{1,0:T(1,128)S(1)}, f32[1,8192]{1,0:T(1,128)}, u32[]{:S(2)}) copy-start(f32[1,8192]{1,0:T(1,128)} %copy-done.6) | copy-start | bytes 98308
  244.9 2.9 %copy-start.3 = (f32[4,2,4,8,2048]{4,3,0,2,1:T(8,128)S(1)}, f32[4,2,4,8,2048]{4,3,0,2,1:T(8,128)}, u32[]{:S(2)}) copy-start(f32[4,2,4,8,2048]{4,3,0,2,1:T(8,128)} %copy.152) | copy-start | bytes 6291460
  266.6 3.2 %copy-start.1 = (bf16[1,2048,512]{2,1,0:T(8,128)(2,1)S(1)}, bf16[1,2048,512]{2,1,0:T(8,128)(2,1)}, u32[]{:S(2)}) copy-start(bf16[1,2048,512]{2,1,0:T(8,128)(2,1)} %param.9) | copy-start | bytes 6291460
Sparse Core Ops, SparseCore 0:
  140.9 46.6 all-gather.2
